TPU v7x, 512 devices: a whole 4x4x16 slice. The times are simulated.
512 devices in a mesh: dp: 16 (over y_lo, x, core), mp: 32 (over z, y_hi).
Axes of the slice: x: 4, y: 4 (y_hi: 2, y_lo: 2; y = y_hi * 2 + y_lo), z: 16, core: 2. Of those that a mesh axis runs over, the one named last changes fastest.
Arguments:
- hidden_states: bfloat16 [8192, 2560], P(('dp', 'mp')), may hold values from -60 to 60
- norm_gain: float32 [2560], replicated, may hold values from 0.5 to 1.5
- head_weight: bfloat16 [2560, 65536], P(None, ('dp', 'mp')), may hold values from -64 to 64
- target_ids: int32 [8192], P(('dp', 'mp')), may hold values from 0 to 65535
- response_mask: int32 [8192], P(('dp', 'mp')), may hold values from 0 to 1, as said below
Outputs:
- token_logprob: float32 [8192], P(('dp', 'mp'))
- token_entropy: float32 [8192], P(('dp', 'mp'))
Inputs may be any that keep to these rules, and one draw needn't show every extreme that they name: `response_mask`: each aligned run of 256 positions is one rollout: a prompt of 0s, then one span of 1s, then padding 0s.
All inputs are finite; a program needn't handle non-finite values.
Results may differ from a plain program's by a relative error of at most 0.0048.
Values may be sent and summed in bfloat16 or wider, within the bound.
No kernel may reach another device: no remote copies, remote signals or barrier semaphores. Data moves between devices by JAX's collectives and lax.ppermute only.
A program may use at most 64 MiB of HBM per device.

v0:
```python
import jax
import jax.numpy as jnp
from jax import lax
from jax.sharding import PartitionSpec as P

lowest_start = -1e30


def combined_all(value, axis, join):
    pieces = jax.tree.map(lambda part: lax.all_gather(part, axis), value)
    head = jax.tree.map(lambda part: part[0], pieces)
    tail = jax.tree.map(lambda part: part[1:], pieces)
    total, _ = lax.scan(lambda total, share: (join(total, share), None), head, tail)
    return total


def combine_stats(earlier, later):
    top_first, sum_first, moment_first, chosen_first = earlier
    top_second, sum_second, moment_second, chosen_second = later
    top_new = jnp.maximum(top_first, top_second)
    factor_first = jnp.exp(top_first - top_new)
    factor_second = jnp.exp(top_second - top_new)
    return (
        top_new,
        sum_first * factor_first + sum_second * factor_second,
        moment_first * factor_first + moment_second * factor_second,
        chosen_first + chosen_second,
    )


def start_stats(row_count):
    zeros = jnp.zeros((row_count,), jnp.float32)
    return (jnp.full((row_count,), lowest_start, jnp.float32), zeros, zeros, zeros)


def add_columns(running, token_rows, token_targets, column_piece, column_ids):
    logits = jnp.dot(token_rows, column_piece, preferred_element_type=jnp.float32)
    piece_top = jnp.max(logits, axis=1)
    shifted = jnp.exp(logits - piece_top[:, None])
    target_hit = token_targets[:, None] == column_ids[None, :]
    piece_stats = (
        piece_top,
        jnp.sum(shifted, axis=1),
        jnp.sum(shifted * logits, axis=1),
        jnp.sum(jnp.where(target_hit, logits, 0.0), axis=1),
    )
    return combine_stats(running, piece_stats)


def local(hidden_states, norm_gain, head_weight, target_ids, response_mask):
    states = hidden_states.astype(jnp.float32)
    mean_square = jnp.mean(states * states, axis=1, keepdims=True)
    normed = (states * lax.rsqrt(mean_square + 1e-06) * norm_gain[None, :]).astype(jnp.bfloat16)
    mp_count = lax.axis_size("mp")
    mp_index = lax.axis_index("mp")
    shard_cols = head_weight.shape[1]
    send_count = normed.shape[0]
    group_states, group_targets = (
        lax.all_gather(normed, "mp", axis=0, tiled=True),
        lax.all_gather(target_ids, "mp", axis=0, tiled=True),
    )
    column_piece = lax.all_gather(head_weight, "dp", axis=1, tiled=True)
    positions = jnp.arange(column_piece.shape[1], dtype=jnp.int32)
    owners = positions // shard_cols
    column_ids = (owners * mp_count + mp_index) * shard_cols + positions % shard_cols
    partial_stats = add_columns(
        start_stats(group_states.shape[0]), group_states, group_targets, column_piece, column_ids
    )
    merged = combined_all(partial_stats, "mp", combine_stats)
    first_row = mp_index * send_count
    top_logit, weight_total, moment, chosen = [
        lax.dynamic_slice_in_dim(member, first_row, send_count) for member in merged
    ]
    log_total = top_logit + jnp.log(weight_total)
    logprob = chosen - log_total
    entropy = log_total - moment / weight_total
    scored = response_mask.astype(jnp.float32)
    return (logprob * scored, entropy * scored)


def solution(mesh):
    return jax.shard_map(
        local,
        mesh=mesh,
        in_specs=(
            P(("dp", "mp"), None),
            P(),
            P(None, ("dp", "mp")),
            P(("dp", "mp")),
            P(("dp", "mp")),
        ),
        out_specs=(P(("dp", "mp")), P(("dp", "mp"))),
        check_vma=False,
    )
```

profile of v0, /device:TPU:16, one launch (start us, length us, event | category | flops | bytes accessed | tf_op | source)
XLA Modules:
  0.0 556.4 jit_solution(13439225483847453185)
XLA Ops:
  7.2 0.0 all-gather.8.cloned.1.call-start
  7.2 1.0 fusion.1
  8.2 1.6 fusion.3
  9.9 0.0 all-gather.8.cloned.1.call-update
  9.9 0.0 all-gather.10.cloned.1.call-start
  9.9 0.7 all-gather.10.cloned.1.call-update
  10.6 1.3 dynamic-slice
  12.6 0.9 dynamic-update-slice
  13.4 30.9 %all-reduce = s32[512]{0:T(512)S(1)} all-reduce(s32[512]{0:T(512)S(1)} %dynamic-update-slice), channel_id=1, replica_groups=mesh['dp'=16,'mp'=32] {'mp'}, use_global_device_ids=true, to_apply=%add | all-reduce | flops 512 | bytes 4096
  44.3 121.9 %all-gather.8.cloned.1.call-done = bf16[512,2560]{1,0:T(8,128)(2,1)} async-done(((bf16[16,2560]{1,0:T(8,128)(2,1)}), bf16[512,2560]{1,0:T(8,128)(2,1)}) %all-gather.8.cloned.1.call-update) | async-done | bytes 2621456 | tf_op jit(solution)/shard_map/all_gather | solution.py:59
  166.3 74.4 %all-gather.10.cloned.1.call-done = bf16[2560,2048]{1,0:T(8,128)(2,1)} async-done(((bf16[2560,128]{1,0:T(8,128)(2,1)}), bf16[2560,2048]{1,0:T(8,128)(2,1)}) %all-gather.10.cloned.1.call-update) | async-done | bytes 10485776 | tf_op jit(solution)/shard_map/all_gather | solution.py:62
  240.7 9.2 %fusion.15 = (f32[512]{0:T(512)S(1)}, f32[512,2048]{1,0:T(8,128)S(1)}) fusion(bf16[512,2560]{1,0:T(8,128)(2,1)} %all-gather.8.cloned.1.call-done, bf16[2560,2048]{1,0:T(8,128)(2,1)} %all-gather.10.cloned.1.call-done), kind=kOutput, calls=%fused_computation.45 | convolution fusion | flops 5369757184 | bytes 17303552 | tf_op jit(solution)/shard_map/dot_general | solution.py:37
  249.9 0.0 copy-start
  249.9 1.9 multiply_reduce_fusion
  251.8 73.0 %all-gather.3 = f32[32,1,512]{2,1,0:T(1,128)S(1)} all-gather(f32[1,1,512]{2,1,0:T(1,128)S(1)} %get-tuple-element.85), channel_id=1, replica_groups=mesh['dp'=16,'mp'=32] {'mp'}, dimensions={0}, use_global_device_ids=true | all-gather | bytes 67584 | tf_op jit(solution)/shard_map/all_gather | solution.py:10
  324.8 75.5 %all-gather.1 = f32[32,1,512]{2,1,0:T(1,128)S(1)} all-gather(f32[1,1,512]{2,1,0:T(1,128)S(1)} %get-tuple-element.87), channel_id=1, replica_groups=mesh['dp'=16,'mp'=32] {'mp'}, dimensions={0}, use_global_device_ids=true | all-gather | bytes 67584 | tf_op jit(solution)/shard_map/all_gather | solution.py:10
  400.3 70.7 %all-gather.2 = f32[32,1,512]{2,1,0:T(1,128)S(1)} all-gather(f32[1,1,512]{2,1,0:T(1,128)S(1)} %get-tuple-element.86), channel_id=1, replica_groups=mesh['dp'=16,'mp'=32] {'mp'}, dimensions={0}, use_global_device_ids=true | all-gather | bytes 67584 | tf_op jit(solution)/shard_map/all_gather | solution.py:10
  471.0 74.2 %all-gather.4 = f32[32,1,512]{2,1,0:T(1,128)S(1)} all-gather(f32[1,1,512]{2,1,0:T(1,128)S(1)} %bitcast.54), channel_id=2, replica_groups=mesh['dp'=16,'mp'=32] {'mp'}, dimensions={0}, use_global_device_ids=true | all-gather | bytes 67584 | tf_op jit(solution)/shard_map/all_gather | solution.py:10
  545.3 3.6 while.16
  549.0 0.0 copy-done
  549.0 0.6 subtract_multiply_fusion
  (202 shorter events, 2.3 us)
Async XLA Ops:
  7.2 159.1 %all-gather.8.cloned.1.call-start = ((), (), s32[]{:S(2)}) async-start(), calls=%async_computation | async-start | bytes 2703360 | tf_op jit(solution)/shard_map/all_gather | solution.py:59
  9.9 230.8 %all-gather.10.cloned.1.call-start = ((), (), s32[]{:S(2)}) async-start(), calls=%async_computation.1 | async-start | bytes 11141120 | tf_op jit(solution)/shard_map/all_gather | solution.py:62
  249.9 299.1 %copy-start = (s32[16]{0:T(128)S(1)}, s32[16]{0:T(128)}, u32[]{:S(2)}) copy-start(s32[16]{0:T(128)} %param.11) | copy-start | bytes 196
Sparse Core Ops, SparseCore 0:
  11.1 155.1 all-gather.7
  168.3 72.2 all-gather.9
where the time goes:
time: 557 us; the launch traced here: 556 us
  blocking collectives  324 us (58%)
  waiting for transfers between devices  197 us (35%)
  between operations  14.8 us (3%)
  matrix products  9.23 us (2%)
  other arithmetic  6.51 us (1%)
    all_gather x4, blocking collectives, combined_all(): pieces = jax.tree.map(lambda part: lax.all_gather(part, axis), value)  293 us
    all_gather x1, waiting for transfers between devices, local(): lax.all_gather(normed, 'mp', axis=0, tiled=True)  122 us
    all_gather x1, waiting for transfers between devices, local(): column_piece = lax.all_gather(head_weight, 'dp', axis=1, tiled=True)  74.4 us
    unnamed x1, blocking collectives  30.9 us
  transfers between devices with their start and end apart: 2, of which 2 were waited for; matrix products, arithmetic and copies ran while one was open for 0% of the time, Pallas kernels for 0%

commit v1 on v0

v1 whole, which is shorter than its diff:
```python
import jax
import jax.numpy as jnp
from jax import lax
from jax.sharding import PartitionSpec as P

id_base = 256


def local(hidden_states, norm_gain, head_weight, target_ids, response_mask):
    states = hidden_states.astype(jnp.float32)
    mean_square = jnp.mean(states * states, axis=1, keepdims=True)
    normed = (states * lax.rsqrt(mean_square + 1e-06) * norm_gain[None, :]).astype(jnp.bfloat16)
    width = normed.shape[1]
    mp_count = lax.axis_size("mp")
    mp_index = lax.axis_index("mp")
    shard_cols = head_weight.shape[1]
    send_count = normed.shape[0]
    id_high = (target_ids // id_base).astype(jnp.bfloat16)
    id_low = (target_ids % id_base).astype(jnp.bfloat16)
    packed = jnp.concatenate([normed, id_high[:, None], id_low[:, None]], axis=1)
    group = lax.all_gather(packed, "mp", axis=0, tiled=True)
    group_states = group[:, :width]
    group_targets = (
        group[:, width].astype(jnp.int32) * id_base + group[:, width + 1].astype(jnp.int32)
    )
    column_piece = lax.all_gather(head_weight, "dp", axis=1, tiled=True)
    positions = jnp.arange(column_piece.shape[1], dtype=jnp.int32)
    owners = positions // shard_cols
    column_ids = (owners * mp_count + mp_index) * shard_cols + positions % shard_cols

    logits = jnp.dot(group_states, column_piece, preferred_element_type=jnp.float32)
    top = jnp.max(logits, axis=1)
    shifted = jnp.exp(logits - top[:, None])
    total = jnp.sum(shifted, axis=1)
    moment = jnp.sum(shifted * logits, axis=1)
    hit = group_targets[:, None] == column_ids[None, :]
    chosen = jnp.sum(jnp.where(hit, logits, 0.0), axis=1)
    part_lse = top + jnp.log(total)
    part_expected = moment / total

    stats = jnp.stack([part_lse, part_expected, chosen], axis=0)
    stats = stats.reshape(3, mp_count, send_count)
    got = lax.all_to_all(stats, "mp", split_axis=1, concat_axis=1, tiled=True)
    lse_parts, expected_parts, chosen_parts = got[0], got[1], got[2]
    top_lse = jnp.max(lse_parts, axis=0)
    log_total = top_lse + jnp.log(jnp.sum(jnp.exp(lse_parts - top_lse[None, :]), axis=0))
    weights = jnp.exp(lse_parts - log_total[None, :])
    expected = jnp.sum(weights * expected_parts, axis=0)
    chosen_logit = jnp.sum(chosen_parts, axis=0)

    scored = response_mask.astype(jnp.float32)
    return ((chosen_logit - log_total) * scored, (log_total - expected) * scored)


def solution(mesh):
    return jax.shard_map(
        local,
        mesh=mesh,
        in_specs=(
            P(("dp", "mp"), None),
            P(),
            P(None, ("dp", "mp")),
            P(("dp", "mp")),
            P(("dp", "mp")),
        ),
        out_specs=(P(("dp", "mp")), P(("dp", "mp"))),
        check_vma=False,
    )
```

time: 557 us -> 292 us (0.52)
  the two profiles are of different devices: /device:TPU:16 before, /device:TPU:2 now
where the time goes in v1:
time: 292 us; the launch traced here: 291 us
  waiting for transfers between devices  230 us (79%)
  blocking collectives  29.5 us (10%)
  between operations  14.1 us (5%)
  matrix products  9.23 us (3%)
  other arithmetic  6.95 us (2%)
    all_gather x1, waiting for transfers between devices, local(): group = lax.all_gather(packed, 'mp', axis=0, tiled=True)  159 us
    all_gather x1, waiting for transfers between devices, local(): column_piece = lax.all_gather(head_weight, 'dp', axis=1, tiled=True)  71.3 us
    all_to_all x1, blocking collectives, local(): got = lax.all_to_all(stats, 'mp', split_axis=1, concat_axis=1, tiled=True)  29.5 us
    dot_general x1, matrix products, local(): jnp.dot(group_states, column_piece, preferred_element_type=jnp.float32)  9.23 us
  transfers between devices with their start and end apart: 2, of which 2 were waited for; matrix products, arithmetic and copies ran while one was open for 0% of the time, Pallas kernels for 0%

profile of v1, /device:TPU:2, one launch (start us, length us, event | category | flops | bytes accessed | tf_op | source)
XLA Modules:
  0.0 291.5 jit_solution(14386886251495838894)
XLA Ops:
  7.2 0.0 all-gather.3.cloned.1.call-start
  7.2 0.7 fusion.18
  7.9 0.1 copy.11
  8.0 0.1 copy.12
  8.1 1.0 fusion.3
  9.1 1.0 fusion.5
  10.1 0.7 concatenate.4
  10.8 0.0 all-gather.3.cloned.1.call-update
  10.8 0.0 all-gather.5.cloned.1.call-start
  10.9 0.7 all-gather.5.cloned.1.call-update
  11.6 158.5 %all-gather.3.cloned.1.call-done = bf16[512,2562]{1,0:T(8,128)(2,1)} async-done(((bf16[16,2562]{1,0:T(8,128)(2,1)}), bf16[512,2562]{1,0:T(8,128)(2,1)}) %all-gather.3.cloned.1.call-update) | async-done | bytes 2623504 | tf_op jit(solution)/shard_map/all_gather | solution.py:21
  170.1 1.2 add_reduce_fusion
  171.3 71.3 %all-gather.5.cloned.1.call-done = bf16[2560,2048]{1,0:T(8,128)(2,1)} async-done(((bf16[2560,128]{1,0:T(8,128)(2,1)}), bf16[2560,2048]{1,0:T(8,128)(2,1)}) %all-gather.5.cloned.1.call-update) | async-done | bytes 10485776 | tf_op jit(solution)/shard_map/all_gather | solution.py:26
  242.6 9.2 %fusion.20 = (f32[512]{0:T(512)S(1)}, f32[512,2048]{1,0:T(8,128)S(1)}) fusion(bf16[2560,2048]{1,0:T(8,128)(2,1)} %all-gather.5.cloned.1.call-done, bf16[512,2562]{1,0:T(8,128)(2,1)} %all-gather.3.cloned.1.call-done), kind=kOutput, calls=%fused_computation.45 | convolution fusion | flops 5369757184 | bytes 17303552 | tf_op jit(solution)/shard_map/dot_general | solution.py:31
  251.8 0.0 copy-start
  251.8 1.8 fusion
  253.7 0.1 add.75
  253.8 0.1 div.43
  253.9 0.1 stack.8
  254.0 29.5 %all_to_all.5 = f32[3,32,16]{2,0,1:T(4,128)S(1)} all-to-all(f32[3,32,16]{2,0,1:T(4,128)S(1)} %copy.13), channel_id=1, replica_groups=mesh['dp'=16,'mp'=32] {'mp'}, dimensions={1} | all-to-all | bytes 12288 | tf_op jit(solution)/shard_map/all_to_all | solution.py:43
  283.5 0.1 fusion.19
  283.6 0.0 copy-done
  283.6 0.5 convert_multiply_fusion.2
  284.1 0.5 subtract_multiply_fusion
  (8 shorter events, 0.2 us)
Async XLA Ops:
  7.2 163.0 %all-gather.3.cloned.1.call-start = ((), (), s32[]{:S(2)}) async-start(), calls=%async_computation.1 | async-start | bytes 2838528 | tf_op jit(solution)/shard_map/all_gather | solution.py:21
  10.8 231.8 %all-gather.5.cloned.1.call-start = ((), (), s32[]{:S(2)}) async-start(), calls=%async_computation.2 | async-start | bytes 11141120 | tf_op jit(solution)/shard_map/all_gather | solution.py:26
  251.8 31.7 %copy-start = (s32[16]{0:T(128)S(1)}, s32[16]{0:T(128)}, u32[]{:S(2)}) copy-start(s32[16]{0:T(128)} %param.9) | copy-start | bytes 196
Sparse Core Ops, SparseCore 0:
  11.1 158.9 all-gather.2
  172.2 70.3 all-gather.4

commit v2 on v1

v2 whole, which is shorter than its diff:
```python
import jax
import jax.numpy as jnp
from jax import lax
from jax.sharding import Mesh, PartitionSpec as P

id_base = 256
dp_axes = ("ylo", "x", "core")
mp_axes = ("z", "yhi")
every = dp_axes + mp_axes


def local(hidden_states, norm_gain, head_weight, target_ids, response_mask):
    states = hidden_states.astype(jnp.float32)
    mean_square = jnp.mean(states * states, axis=1, keepdims=True)
    normed = (states * lax.rsqrt(mean_square + 1e-06) * norm_gain[None, :]).astype(jnp.bfloat16)
    width = normed.shape[1]
    mp_count = lax.axis_size(mp_axes)
    mp_index = lax.axis_index(mp_axes)
    shard_cols = head_weight.shape[1]
    send_count = normed.shape[0]
    id_high = (target_ids // id_base).astype(jnp.bfloat16)
    id_low = (target_ids % id_base).astype(jnp.bfloat16)
    packed = jnp.concatenate([normed, id_high[:, None], id_low[:, None]], axis=1)
    pair = lax.all_gather(packed, "yhi", axis=0, tiled=True)
    group = lax.all_gather(pair, "z", axis=0, tiled=True)
    group_states = group[:, :width]
    group_targets = (
        group[:, width].astype(jnp.int32) * id_base + group[:, width + 1].astype(jnp.int32)
    )
    column_piece = lax.all_gather(head_weight, dp_axes, axis=1, tiled=True)
    positions = jnp.arange(column_piece.shape[1], dtype=jnp.int32)
    owners = positions // shard_cols
    column_ids = (owners * mp_count + mp_index) * shard_cols + positions % shard_cols

    logits = jnp.dot(group_states, column_piece, preferred_element_type=jnp.float32)
    top = jnp.max(logits, axis=1)
    shifted = jnp.exp(logits - top[:, None])
    total = jnp.sum(shifted, axis=1)
    moment = jnp.sum(shifted * logits, axis=1)
    hit = group_targets[:, None] == column_ids[None, :]
    chosen = jnp.sum(jnp.where(hit, logits, 0.0), axis=1)
    part_lse = top + jnp.log(total)
    part_expected = moment / total

    stats = jnp.stack([part_lse, part_expected, chosen], axis=0)
    stats = stats.reshape(3, mp_count, send_count)
    got = lax.all_to_all(stats, mp_axes, split_axis=1, concat_axis=1, tiled=True)
    lse_parts, expected_parts, chosen_parts = got[0], got[1], got[2]
    top_lse = jnp.max(lse_parts, axis=0)
    log_total = top_lse + jnp.log(jnp.sum(jnp.exp(lse_parts - top_lse[None, :]), axis=0))
    weights = jnp.exp(lse_parts - log_total[None, :])
    expected = jnp.sum(weights * expected_parts, axis=0)
    chosen_logit = jnp.sum(chosen_parts, axis=0)

    scored = response_mask.astype(jnp.float32)
    return ((chosen_logit - log_total) * scored, (log_total - expected) * scored)


def split_mesh(mesh):
    dp_size, mp_size = mesh.devices.shape
    shape = (2, dp_size // 4, 2, mp_size // 2, 2)
    return Mesh(mesh.devices.reshape(shape), every)


def solution(mesh):
    return jax.shard_map(
        local,
        mesh=split_mesh(mesh),
        in_specs=(
            P(every, None),
            P(),
            P(None, every),
            P(every),
            P(every),
        ),
        out_specs=(P(every), P(every)),
        check_vma=False,
    )
```

time: 292 us -> 220 us (0.75)
  waiting for transfers between devices: 230 us -> 153 us
  blocking collectives: 29.5 us -> 36.2 us
    all_gather x2, waiting for transfers between devices: 230 us -> 152 us  [the longest x1 78.2 us: local(): group = lax.all_gather(pair, 'z', axis=0, tiled=True)]
    all_gather x0 -> x1, blocking collectives: none -> 6.75 us  [local(): pair = lax.all_gather(packed, 'yhi', axis=0, tiled=True)]
  transfers between devices with their start and end apart: 2 -> 2, of which waited for: 2 -> 2; matrix products, arithmetic and copies ran while one was open for 0% -> 1% of each run, Pallas kernels for 0% -> 0%
where the time goes in v2:
time: 220 us
  waiting for transfers between devices  153 us (70%)
  blocking collectives  36.2 us (16%)
  between operations  14.1 us (6%)
  matrix products  9.23 us (4%)
  other arithmetic  6.95 us (3%)
    all_gather x1, waiting for transfers between devices, local(): group = lax.all_gather(pair, 'z', axis=0, tiled=True)  78.2 us
    all_gather x1, waiting for transfers between devices, local(): column_piece = lax.all_gather(head_weight, dp_axes, axis=1, tiled=True)  73.9 us
    all_to_all x1, blocking collectives, local(): lax.all_to_all(stats, mp_axes, split_axis=1, concat_axis=1, tiled=True)  29.5 us
    dot_general x1, matrix products, local(): jnp.dot(group_states, column_piece, preferred_element_type=jnp.float32)  9.23 us
    all_gather x1, blocking collectives, local(): pair = lax.all_gather(packed, 'yhi', axis=0, tiled=True)  6.75 us
  transfers between devices with their start and end apart: 2, of which 2 were waited for; matrix products, arithmetic and copies ran while one was open for 1% of the time, Pallas kernels for 0%

profile of v2, /device:TPU:2, one launch (start us, length us, event | category | flops | bytes accessed | tf_op | source)
XLA Modules:
  0.0 219.9 jit_solution(7352655338182290467)
XLA Ops:
  7.2 0.0 all-gather.3.cloned.1.call-start
  7.2 0.7 fusion.18
  7.9 0.1 copy.11
  8.0 0.1 copy.12
  8.1 1.0 fusion.3
  9.1 1.0 fusion.5
  10.1 0.1 concatenate.4
  10.2 6.8 %all_gather.9 = bf16[32,2562]{1,0:T(8,128)(2,1)} all-gather(bf16[16,2562]{1,0:T(8,128)(2,1)S(1)} %concatenate.4), channel_id=1, replica_groups=mesh['ylo'=2,'x'=4,'core'=2,'z'=16,'yhi'=2] {'yhi'}, dimensions={0}, use_global_device_ids=true | all-gather | bytes 245952 | tf_op jit(solution)/shard_map/all_gather | solution.py:24
  16.9 0.0 all-gather.3.cloned.1.call-update
  17.0 0.0 all-gather.5.cloned.1.call-start
  17.0 0.7 all-gather.5.cloned.1.call-update
  17.7 78.2 %all-gather.3.cloned.1.call-done = bf16[512,2562]{1,0:T(8,128)(2,1)} async-done(((bf16[32,2562]{1,0:T(8,128)(2,1)}), bf16[512,2562]{1,0:T(8,128)(2,1)}) %all-gather.3.cloned.1.call-update) | async-done | bytes 2623504 | tf_op jit(solution)/shard_map/all_gather | solution.py:25
  96.0 1.2 add_reduce_fusion
  97.2 73.9 %all-gather.5.cloned.1.call-done = bf16[2560,2048]{1,0:T(8,128)(2,1)} async-done(((bf16[2560,128]{1,0:T(8,128)(2,1)}), bf16[2560,2048]{1,0:T(8,128)(2,1)}) %all-gather.5.cloned.1.call-update) | async-done | bytes 10485776 | tf_op jit(solution)/shard_map/all_gather | solution.py:30
  171.0 9.2 %fusion.20 = (f32[512]{0:T(512)S(1)}, f32[512,2048]{1,0:T(8,128)S(1)}) fusion(bf16[2560,2048]{1,0:T(8,128)(2,1)} %all-gather.5.cloned.1.call-done, bf16[512,2562]{1,0:T(8,128)(2,1)} %all-gather.3.cloned.1.call-done), kind=kOutput, calls=%fused_computation.45 | convolution fusion | flops 5369757184 | bytes 17303552 | tf_op jit(solution)/shard_map/dot_general | solution.py:35
  180.3 0.0 copy-start
  180.3 1.8 fusion
  182.1 0.1 add.78
  182.2 0.1 div.43
  182.3 0.1 stack.8
  182.4 29.5 %all_to_all.5 = f32[3,32,16]{2,0,1:T(4,128)S(1)} all-to-all(f32[3,32,16]{2,0,1:T(4,128)S(1)} %copy.13), channel_id=1, replica_groups=mesh['ylo'=2,'x'=4,'core'=2,'z'=16,'yhi'=2] {'z','yhi'}, dimensions={1} | all-to-all | bytes 12288 | tf_op jit(solution)/shard_map/all_to_all | solution.py:47
  211.9 0.1 fusion.19
  212.0 0.0 copy-done
  212.0 0.5 convert_multiply_fusion.2
  212.6 0.5 subtract_multiply_fusion
  (8 shorter events, 0.2 us)
Async XLA Ops:
  7.2 88.8 %all-gather.3.cloned.1.call-start = ((), (), s32[]{:S(2)}) async-start(), calls=%async_computation.1 | async-start | bytes 2924544 | tf_op jit(solution)/shard_map/all_gather | solution.py:25
  17.0 154.1 %all-gather.5.cloned.1.call-start = ((), (), s32[]{:S(2)}) async-start(), calls=%async_computation.2 | async-start | bytes 11141120 | tf_op jit(solution)/shard_map/all_gather | solution.py:30
  180.3 31.7 %copy-start = (s32[16]{0:T(128)S(1)}, s32[16]{0:T(128)}, u32[]{:S(2)}) copy-start(s32[16]{0:T(128)} %param.9) | copy-start | bytes 196
Sparse Core Ops, SparseCore 0:
  17.1 78.8 all-gather.2
  98.0 72.9 all-gather.4

commit v3 on v2

--- a/solution.py
+++ b/solution.py
@@ -7,6 +7,11 @@
 dp_axes = ("ylo", "x", "core")
 mp_axes = ("z", "yhi")
 every = dp_axes + mp_axes
+
+
+def shift(value, axis, step):
+    count = lax.axis_size(axis)
+    return lax.ppermute(value, axis, [(i, (i + step) % count) for i in range(count)])
 
 
 def local(hidden_states, norm_gain, head_weight, target_ids, response_mask):
@@ -21,8 +26,21 @@
     id_high = (target_ids // id_base).astype(jnp.bfloat16)
     id_low = (target_ids % id_base).astype(jnp.bfloat16)
     packed = jnp.concatenate([normed, id_high[:, None], id_low[:, None]], axis=1)
-    pair = lax.all_gather(packed, "yhi", axis=0, tiled=True)
-    group = lax.all_gather(pair, "z", axis=0, tiled=True)
+    z_count = lax.axis_size("z")
+    z_index = lax.axis_index("z")
+    yhi_index = lax.axis_index("yhi")
+    pair = jnp.concatenate([packed, shift(packed, "yhi", 1)], axis=0)
+    ahead = pair
+    behind = pair
+    blocks = [pair]
+    returning = []
+    for _ in range(z_count // 2 - 1):
+        ahead = shift(ahead, "z", 1)
+        behind = shift(behind, "z", -1)
+        blocks.append(ahead)
+        returning.append(behind)
+    blocks.append(shift(ahead, "z", 1))
+    group = jnp.concatenate(blocks + returning[::-1], axis=0)
     group_states = group[:, :width]
     group_targets = (
         group[:, width].astype(jnp.int32) * id_base + group[:, width + 1].astype(jnp.int32)
@@ -44,6 +62,9 @@
 
     stats = jnp.stack([part_lse, part_expected, chosen], axis=0)
     stats = stats.reshape(3, mp_count, send_count)
+    owner = jnp.arange(mp_count, dtype=jnp.int32)
+    source = ((z_index - owner // 2) % z_count) * 2 + (owner % 2 + yhi_index) % 2
+    stats = jnp.take(stats, source, axis=1)
     got = lax.all_to_all(stats, mp_axes, split_axis=1, concat_axis=1, tiled=True)
     lse_parts, expected_parts, chosen_parts = got[0], got[1], got[2]
     top_lse = jnp.max(lse_parts, axis=0)

time: 220 us -> 144 us (0.65)
  the two profiles are of different devices: /device:TPU:2 before, /device:TPU:4 now
where the time goes in v3:
time: 144 us; the launch traced here: 143 us
  starting transfers between devices  63.5 us (44%)
  blocking collectives  26.9 us (19%)
  waiting for transfers between devices  22 us (15%)
  between operations  14.3 us (10%)
  matrix products  8.41 us (6%)
  other arithmetic  6.34 us (4%)
  local copies, waits for them, and re-layouts  1.46 us (1%)
    ppermute x16, starting transfers between devices, shift(): lax.ppermute(value, axis, [(i, (i + step) % count) for i in range(count)])  63.5 us
    all_to_all x1, blocking collectives, local(): lax.all_to_all(stats, mp_axes, split_axis=1, concat_axis=1, tiled=True)  26.9 us
    ppermute x16, waiting for transfers between devices, shift(): lax.ppermute(value, axis, [(i, (i + step) % count) for i in range(count)])  21.4 us
    dot_general x1, matrix products, local(): jnp.dot(group_states, column_piece, preferred_element_type=jnp.float32)  8.41 us
  transfers between devices with their start and end apart: 17, of which 10 were waited for; matrix products, arithmetic and copies ran while one was open for 3% of the time, Pallas kernels for 0%

profile of v3, /device:TPU:4, one launch (start us, length us, event | category | flops | bytes accessed | tf_op | source)
XLA Modules:
  0.0 143.0 jit_solution(16324608831109021824)
XLA Ops:
  7.2 0.0 all-gather.2.cloned.1.call-start
  7.2 0.7 all-gather.2.cloned.1.call-update
  7.9 0.7 fusion.25
  8.6 0.1 copy.23
  8.7 0.1 copy.24
  8.8 1.0 fusion.3
  9.8 1.0 fusion.5
  10.8 0.1 concatenate.11
  10.9 5.1 %collective-permute-start = (bf16[16,2562]{1,0:T(8,128)(2,1)S(1)}, bf16[16,2562]{1,0:T(8,128)(2,1)S(1)}, u32[]{:S(2)}, u32[]{:S(2)}) collective-permute-start(bf16[16,2562]{1,0:T(8,128)(2,1)S(1)} %concatenate.11), channel_id=1, source_target_pairs={{0,1},{1,0},{2,3},{3,2},{4,5},{5,4},{6,7},{7,6},{8,9},{9,8},{10,11... | collective-permute-start | bytes 245960 | tf_op jit(solution)/shard_map/ppermute | solution.py:14
  16.1 2.7 %collective-permute-done = bf16[16,2562]{1,0:T(8,128)(2,1)S(1)} collective-permute-done((bf16[16,2562]{1,0:T(8,128)(2,1)S(1)}, bf16[16,2562]{1,0:T(8,128)(2,1)S(1)}, u32[]{:S(2)}, u32[]{:S(2)}) %collective-permute-start) | collective-permute-done | bytes 82016 | tf_op jit(solution)/shard_map/ppermute | solution.py:14
  18.8 3.8 %collective-permute-start.1 = (bf16[32,2562]{1,0:T(8,128)(2,1)S(1)}, bf16[32,2562]{1,0:T(8,128)(2,1)S(1)}, u32[]{:S(2)}, u32[]{:S(2)}) collective-permute-start(bf16[32,2562]{1,0:T(8,128)(2,1)S(1)} %pad_maximum_fusion), channel_id=1, source_target_pairs={{0,2},{2,4},{4,6},{6,8},{8,10},{10,12},{12,14},{14,16},{16,18},{18... | collective-permute-start | bytes 491912 | tf_op jit(solution)/shard_map/ppermute | solution.py:14
  22.6 9.5 %collective-permute-start.9 = (bf16[32,2562]{1,0:T(8,128)(2,1)S(1)}, bf16[32,2562]{1,0:T(8,128)(2,1)S(1)}, u32[]{:S(2)}, u32[]{:S(2)}) collective-permute-start(bf16[32,2562]{1,0:T(8,128)(2,1)S(1)} %pad_maximum_fusion), channel_id=1, source_target_pairs={{0,30},{2,0},{4,2},{6,4},{8,6},{10,8},{12,10},{14,12},{16,14},{18,... | collective-permute-start | bytes 491912 | tf_op jit(solution)/shard_map/ppermute | solution.py:14
  32.1 1.4 collective-permute-done.1
  33.5 1.9 %collective-permute-start.2 = (bf16[32,2562]{1,0:T(8,128)(2,1)S(1)}, bf16[32,2562]{1,0:T(8,128)(2,1)S(1)}, u32[]{:S(2)}, u32[]{:S(2)}) collective-permute-start(bf16[32,2562]{1,0:T(8,128)(2,1)S(1)} %collective-permute-done.1), channel_id=1, source_target_pairs={{0,2},{2,4},{4,6},{6,8},{8,10},{10,12},{12,14},{14,16},{16,18},{18... | collective-permute-start | bytes 491912 | tf_op jit(solution)/shard_map/ppermute | solution.py:14
  35.5 5.1 %collective-permute-start.10 = (bf16[32,2562]{1,0:T(8,128)(2,1)S(1)}, bf16[32,2562]{1,0:T(8,128)(2,1)S(1)}, u32[]{:S(2)}, u32[]{:S(2)}) collective-permute-start(bf16[32,2562]{1,0:T(8,128)(2,1)S(1)} %collective-permute-done.9), channel_id=1, source_target_pairs={{0,30},{2,0},{4,2},{6,4},{8,6},{10,8},{12,10},{14,12},{16,14},{18,... | collective-permute-start | bytes 491912 | tf_op jit(solution)/shard_map/ppermute | solution.py:14
  40.6 1.4 collective-permute-done.2
  42.0 1.9 %collective-permute-start.3 = (bf16[32,2562]{1,0:T(8,128)(2,1)S(1)}, bf16[32,2562]{1,0:T(8,128)(2,1)S(1)}, u32[]{:S(2)}, u32[]{:S(2)}) collective-permute-start(bf16[32,2562]{1,0:T(8,128)(2,1)S(1)} %collective-permute-done.2), channel_id=1, source_target_pairs={{0,2},{2,4},{4,6},{6,8},{8,10},{10,12},{12,14},{14,16},{16,18},{18... | collective-permute-start | bytes 491912 | tf_op jit(solution)/shard_map/ppermute | solution.py:14
  44.0 5.1 %collective-permute-start.11 = (bf16[32,2562]{1,0:T(8,128)(2,1)S(1)}, bf16[32,2562]{1,0:T(8,128)(2,1)S(1)}, u32[]{:S(2)}, u32[]{:S(2)}) collective-permute-start(bf16[32,2562]{1,0:T(8,128)(2,1)S(1)} %collective-permute-done.10), channel_id=1, source_target_pairs={{0,30},{2,0},{4,2},{6,4},{8,6},{10,8},{12,10},{14,12},{16,14},{18,... | collective-permute-start | bytes 491912 | tf_op jit(solution)/shard_map/ppermute | solution.py:14
  49.1 1.4 collective-permute-done.3
  50.5 1.9 %collective-permute-start.4 = (bf16[32,2562]{1,0:T(8,128)(2,1)S(1)}, bf16[32,2562]{1,0:T(8,128)(2,1)S(1)}, u32[]{:S(2)}, u32[]{:S(2)}) collective-permute-start(bf16[32,2562]{1,0:T(8,128)(2,1)S(1)} %collective-permute-done.3), channel_id=1, source_target_pairs={{0,2},{2,4},{4,6},{6,8},{8,10},{10,12},{12,14},{14,16},{16,18},{18... | collective-permute-start | bytes 491912 | tf_op jit(solution)/shard_map/ppermute | solution.py:14
  52.5 5.1 %collective-permute-start.12 = (bf16[32,2562]{1,0:T(8,128)(2,1)S(1)}, bf16[32,2562]{1,0:T(8,128)(2,1)S(1)}, u32[]{:S(2)}, u32[]{:S(2)}) collective-permute-start(bf16[32,2562]{1,0:T(8,128)(2,1)S(1)} %collective-permute-done.11), channel_id=1, source_target_pairs={{0,30},{2,0},{4,2},{6,4},{8,6},{10,8},{12,10},{14,12},{16,14},{18,... | collective-permute-start | bytes 491912 | tf_op jit(solution)/shard_map/ppermute | solution.py:14
  57.6 1.4 collective-permute-done.4
  59.0 1.9 %collective-permute-start.5 = (bf16[32,2562]{1,0:T(8,128)(2,1)S(1)}, bf16[32,2562]{1,0:T(8,128)(2,1)S(1)}, u32[]{:S(2)}, u32[]{:S(2)}) collective-permute-start(bf16[32,2562]{1,0:T(8,128)(2,1)S(1)} %collective-permute-done.4), channel_id=1, source_target_pairs={{0,2},{2,4},{4,6},{6,8},{8,10},{10,12},{12,14},{14,16},{16,18},{18... | collective-permute-start | bytes 491912 | tf_op jit(solution)/shard_map/ppermute | solution.py:14
  61.0 5.4 %collective-permute-start.13 = (bf16[32,2562]{1,0:T(8,128)(2,1)S(1)}, bf16[32,2562]{1,0:T(8,128)(2,1)S(1)}, u32[]{:S(2)}, u32[]{:S(2)}) collective-permute-start(bf16[32,2562]{1,0:T(8,128)(2,1)S(1)} %collective-permute-done.12), channel_id=1, source_target_pairs={{0,30},{2,0},{4,2},{6,4},{8,6},{10,8},{12,10},{14,12},{16,14},{18,... | collective-permute-start | bytes 491912 | tf_op jit(solution)/shard_map/ppermute | solution.py:14
  66.4 2.3 %collective-permute-done.5 = bf16[32,2562]{1,0:T(8,128)(2,1)S(1)} collective-permute-done((bf16[32,2562]{1,0:T(8,128)(2,1)S(1)}, bf16[32,2562]{1,0:T(8,128)(2,1)S(1)}, u32[]{:S(2)}, u32[]{:S(2)}) %collective-permute-start.5) | collective-permute-done | bytes 164000 | tf_op jit(solution)/shard_map/ppermute | solution.py:14
  68.6 1.9 %collective-permute-start.6 = (bf16[32,2562]{1,0:T(8,128)(2,1)S(1)}, bf16[32,2562]{1,0:T(8,128)(2,1)S(1)}, u32[]{:S(2)}, u32[]{:S(2)}) collective-permute-start(bf16[32,2562]{1,0:T(8,128)(2,1)S(1)} %collective-permute-done.5), channel_id=1, source_target_pairs={{0,2},{2,4},{4,6},{6,8},{8,10},{10,12},{12,14},{14,16},{16,18},{18... | collective-permute-start | bytes 491912 | tf_op jit(solution)/shard_map/ppermute | solution.py:14
  70.6 0.1 collective-permute-done.13
  70.6 5.6 %collective-permute-start.14 = (bf16[32,2562]{1,0:T(8,128)(2,1)S(1)}, bf16[32,2562]{1,0:T(8,128)(2,1)S(1)}, u32[]{:S(2)}, u32[]{:S(2)}) collective-permute-start(bf16[32,2562]{1,0:T(8,128)(2,1)S(1)} %collective-permute-done.13), channel_id=1, source_target_pairs={{0,30},{2,0},{4,2},{6,4},{8,6},{10,8},{12,10},{14,12},{16,14},{18,... | collective-permute-start | bytes 491912 | tf_op jit(solution)/shard_map/ppermute | solution.py:14
  76.2 2.3 %collective-permute-done.6 = bf16[32,2562]{1,0:T(8,128)(2,1)S(1)} collective-permute-done((bf16[32,2562]{1,0:T(8,128)(2,1)S(1)}, bf16[32,2562]{1,0:T(8,128)(2,1)S(1)}, u32[]{:S(2)}, u32[]{:S(2)}) %collective-permute-start.6) | collective-permute-done | bytes 164000 | tf_op jit(solution)/shard_map/ppermute | solution.py:14
  78.6 1.9 %collective-permute-start.7 = (bf16[32,2562]{1,0:T(8,128)(2,1)S(1)}, bf16[32,2562]{1,0:T(8,128)(2,1)S(1)}, u32[]{:S(2)}, u32[]{:S(2)}) collective-permute-start(bf16[32,2562]{1,0:T(8,128)(2,1)S(1)} %collective-permute-done.6), channel_id=1, source_target_pairs={{0,2},{2,4},{4,6},{6,8},{8,10},{10,12},{12,14},{14,16},{16,18},{18... | collective-permute-start | bytes 491912 | tf_op jit(solution)/shard_map/ppermute | solution.py:14
  80.5 5.4 %collective-permute-start.15 = (bf16[32,2562]{1,0:T(8,128)(2,1)S(1)}, bf16[32,2562]{1,0:T(8,128)(2,1)S(1)}, u32[]{:S(2)}, u32[]{:S(2)}) collective-permute-start(bf16[32,2562]{1,0:T(8,128)(2,1)S(1)} %collective-permute-done.14), channel_id=1, source_target_pairs={{0,30},{2,0},{4,2},{6,4},{8,6},{10,8},{12,10},{14,12},{16,14},{18,... | collective-permute-start | bytes 491912 | tf_op jit(solution)/shard_map/ppermute | solution.py:14
  85.9 1.8 %collective-permute-done.7 = bf16[32,2562]{1,0:T(8,128)(2,1)S(1)} collective-permute-done((bf16[32,2562]{1,0:T(8,128)(2,1)S(1)}, bf16[32,2562]{1,0:T(8,128)(2,1)S(1)}, u32[]{:S(2)}, u32[]{:S(2)}) %collective-permute-start.7) | collective-permute-done | bytes 164000 | tf_op jit(solution)/shard_map/ppermute | solution.py:14
  87.7 1.9 %collective-permute-start.8 = (bf16[32,2562]{1,0:T(8,128)(2,1)S(1)}, bf16[32,2562]{1,0:T(8,128)(2,1)S(1)}, u32[]{:S(2)}, u32[]{:S(2)}) collective-permute-start(bf16[32,2562]{1,0:T(8,128)(2,1)S(1)} %collective-permute-done.7), channel_id=1, source_target_pairs={{0,2},{2,4},{4,6},{6,8},{8,10},{10,12},{12,14},{14,16},{16,18},{18... | collective-permute-start | bytes 491912 | tf_op jit(solution)/shard_map/ppermute | solution.py:14
  89.6 6.6 %collective-permute-done.8 = bf16[32,2562]{1,0:T(8,128)(2,1)S(1)} collective-permute-done((bf16[32,2562]{1,0:T(8,128)(2,1)S(1)}, bf16[32,2562]{1,0:T(8,128)(2,1)S(1)}, u32[]{:S(2)}, u32[]{:S(2)}) %collective-permute-start.8) | collective-permute-done | bytes 164000 | tf_op jit(solution)/shard_map/ppermute | solution.py:14
  96.4 0.2 add_reduce_fusion
  96.6 0.0 all-gather.2.cloned.1.call-done
  96.6 8.4 %fusion.33 = (f32[512]{0:T(512)S(1)}, f32[512,2048]{1,0:T(8,128)S(1)}) fusion(bf16[2560,2048]{1,0:T(8,128)(2,1)} %all-gather.2.cloned.1.call-done, bf16[512,2562]{1,0:T(8,128)(2,1)S(1)} %constant_dynamic-update-slice_fusion), kind=kOutput, calls=%fused_computation.104 | convolution fusion | flops 5369757184 | bytes 17303552 | tf_op jit(solution)/shard_map/dot_general | solution.py:53
  105.1 2.0 %fusion = (f32[512]{0:T(512)S(1)}, f32[512]{0:T(512)S(1)}, f32[512]{0:T(512)S(1)}) fusion(f32[512,2048]{1,0:T(8,128)S(1)} %get-tuple-element.15, f32[512]{0:T(512)S(1)} %get-tuple-element.14, s32[2048]{0:T(1024)S(1)} %fusion.15, s32[512]{0:T(512)S(1)} %add_reduce_fusion), kind=kLoop, calls=%fused_computation.4 | loop fusion | flops 7338496 | bytes 4212736 | tf_op jit(solution)/shard_map/reduce_sum | solution.py:56
  107.1 0.1 add.197
  107.1 0.1 div.52
  107.2 0.1 stack.8
  107.3 0.1 pad_maximum_fusion.1
  107.4 0.6 gather_fusion
  108.0 0.1 select_bitcast_fusion
  108.1 26.9 %all_to_all.5 = f32[3,32,16]{2,0,1:T(4,128)S(1)} all-to-all(f32[3,32,16]{2,0,1:T(4,128)S(1)} %select_bitcast_fusion), channel_id=1, replica_groups=mesh['ylo'=2,'x'=4,'core'=2,'z'=16,'yhi'=2] {'z','yhi'}, dimensions={1} | all-to-all | bytes 12288 | tf_op jit(solution)/shard_map/all_to_all | solution.py:68
  134.9 0.1 fusion.32
  135.1 0.5 convert_multiply_fusion.2
  135.6 0.5 subtract_multiply_fusion
  (35 shorter events, 0.5 us)
Async XLA Ops:
  7.2 89.5 %all-gather.2.cloned.1.call-start = ((), (), s32[]{:S(2)}) async-start(), calls=%async_computation.1 | async-start | bytes 11141120 | tf_op jit(solution)/shard_map/all_gather | solution.py:48
  10.9 7.9 %collective-permute-start = (bf16[16,2562]{1,0:T(8,128)(2,1)S(1)}, bf16[16,2562]{1,0:T(8,128)(2,1)S(1)}, u32[]{:S(2)}, u32[]{:S(2)}) collective-permute-start(bf16[16,2562]{1,0:T(8,128)(2,1)S(1)} %concatenate.11), channel_id=1, source_target_pairs={{0,1},{1,0},{2,3},{3,2},{4,5},{5,4},{6,7},{7,6},{8,9},{9,8},{10,11... | collective-permute-start | bytes 245960 | tf_op jit(solution)/shard_map/ppermute | solution.py:14
  18.8 14.8 %collective-permute-start.1 = (bf16[32,2562]{1,0:T(8,128)(2,1)S(1)}, bf16[32,2562]{1,0:T(8,128)(2,1)S(1)}, u32[]{:S(2)}, u32[]{:S(2)}) collective-permute-start(bf16[32,2562]{1,0:T(8,128)(2,1)S(1)} %pad_maximum_fusion), channel_id=1, source_target_pairs={{0,2},{2,4},{4,6},{6,8},{8,10},{10,12},{12,14},{14,16},{16,18},{18... | collective-permute-start | bytes 491912 | tf_op jit(solution)/shard_map/ppermute | solution.py:14
  22.6 12.9 %collective-permute-start.9 = (bf16[32,2562]{1,0:T(8,128)(2,1)S(1)}, bf16[32,2562]{1,0:T(8,128)(2,1)S(1)}, u32[]{:S(2)}, u32[]{:S(2)}) collective-permute-start(bf16[32,2562]{1,0:T(8,128)(2,1)S(1)} %pad_maximum_fusion), channel_id=1, source_target_pairs={{0,30},{2,0},{4,2},{6,4},{8,6},{10,8},{12,10},{14,12},{16,14},{18,... | collective-permute-start | bytes 491912 | tf_op jit(solution)/shard_map/ppermute | solution.py:14
  33.5 8.5 %collective-permute-start.2 = (bf16[32,2562]{1,0:T(8,128)(2,1)S(1)}, bf16[32,2562]{1,0:T(8,128)(2,1)S(1)}, u32[]{:S(2)}, u32[]{:S(2)}) collective-permute-start(bf16[32,2562]{1,0:T(8,128)(2,1)S(1)} %collective-permute-done.1), channel_id=1, source_target_pairs={{0,2},{2,4},{4,6},{6,8},{8,10},{10,12},{12,14},{14,16},{16,18},{18... | collective-permute-start | bytes 491912 | tf_op jit(solution)/shard_map/ppermute | solution.py:14
  35.5 8.5 %collective-permute-start.10 = (bf16[32,2562]{1,0:T(8,128)(2,1)S(1)}, bf16[32,2562]{1,0:T(8,128)(2,1)S(1)}, u32[]{:S(2)}, u32[]{:S(2)}) collective-permute-start(bf16[32,2562]{1,0:T(8,128)(2,1)S(1)} %collective-permute-done.9), channel_id=1, source_target_pairs={{0,30},{2,0},{4,2},{6,4},{8,6},{10,8},{12,10},{14,12},{16,14},{18,... | collective-permute-start | bytes 491912 | tf_op jit(solution)/shard_map/ppermute | solution.py:14
  42.0 8.5 %collective-permute-start.3 = (bf16[32,2562]{1,0:T(8,128)(2,1)S(1)}, bf16[32,2562]{1,0:T(8,128)(2,1)S(1)}, u32[]{:S(2)}, u32[]{:S(2)}) collective-permute-start(bf16[32,2562]{1,0:T(8,128)(2,1)S(1)} %collective-permute-done.2), channel_id=1, source_target_pairs={{0,2},{2,4},{4,6},{6,8},{8,10},{10,12},{12,14},{14,16},{16,18},{18... | collective-permute-start | bytes 491912 | tf_op jit(solution)/shard_map/ppermute | solution.py:14
  44.0 8.5 %collective-permute-start.11 = (bf16[32,2562]{1,0:T(8,128)(2,1)S(1)}, bf16[32,2562]{1,0:T(8,128)(2,1)S(1)}, u32[]{:S(2)}, u32[]{:S(2)}) collective-permute-start(bf16[32,2562]{1,0:T(8,128)(2,1)S(1)} %collective-permute-done.10), channel_id=1, source_target_pairs={{0,30},{2,0},{4,2},{6,4},{8,6},{10,8},{12,10},{14,12},{16,14},{18,... | collective-permute-start | bytes 491912 | tf_op jit(solution)/shard_map/ppermute | solution.py:14
  50.5 8.5 %collective-permute-start.4 = (bf16[32,2562]{1,0:T(8,128)(2,1)S(1)}, bf16[32,2562]{1,0:T(8,128)(2,1)S(1)}, u32[]{:S(2)}, u32[]{:S(2)}) collective-permute-start(bf16[32,2562]{1,0:T(8,128)(2,1)S(1)} %collective-permute-done.3), channel_id=1, source_target_pairs={{0,2},{2,4},{4,6},{6,8},{8,10},{10,12},{12,14},{14,16},{16,18},{18... | collective-permute-start | bytes 491912 | tf_op jit(solution)/shard_map/ppermute | solution.py:14
  52.5 8.5 %collective-permute-start.12 = (bf16[32,2562]{1,0:T(8,128)(2,1)S(1)}, bf16[32,2562]{1,0:T(8,128)(2,1)S(1)}, u32[]{:S(2)}, u32[]{:S(2)}) collective-permute-start(bf16[32,2562]{1,0:T(8,128)(2,1)S(1)} %collective-permute-done.11), channel_id=1, source_target_pairs={{0,30},{2,0},{4,2},{6,4},{8,6},{10,8},{12,10},{14,12},{16,14},{18,... | collective-permute-start | bytes 491912 | tf_op jit(solution)/shard_map/ppermute | solution.py:14
  59.0 9.6 %collective-permute-start.5 = (bf16[32,2562]{1,0:T(8,128)(2,1)S(1)}, bf16[32,2562]{1,0:T(8,128)(2,1)S(1)}, u32[]{:S(2)}, u32[]{:S(2)}) collective-permute-start(bf16[32,2562]{1,0:T(8,128)(2,1)S(1)} %collective-permute-done.4), channel_id=1, source_target_pairs={{0,2},{2,4},{4,6},{6,8},{8,10},{10,12},{12,14},{14,16},{16,18},{18... | collective-permute-start | bytes 491912 | tf_op jit(solution)/shard_map/ppermute | solution.py:14
  61.0 9.6 %collective-permute-start.13 = (bf16[32,2562]{1,0:T(8,128)(2,1)S(1)}, bf16[32,2562]{1,0:T(8,128)(2,1)S(1)}, u32[]{:S(2)}, u32[]{:S(2)}) collective-permute-start(bf16[32,2562]{1,0:T(8,128)(2,1)S(1)} %collective-permute-done.12), channel_id=1, source_target_pairs={{0,30},{2,0},{4,2},{6,4},{8,6},{10,8},{12,10},{14,12},{16,14},{18,... | collective-permute-start | bytes 491912 | tf_op jit(solution)/shard_map/ppermute | solution.py:14
  68.6 9.9 %collective-permute-start.6 = (bf16[32,2562]{1,0:T(8,128)(2,1)S(1)}, bf16[32,2562]{1,0:T(8,128)(2,1)S(1)}, u32[]{:S(2)}, u32[]{:S(2)}) collective-permute-start(bf16[32,2562]{1,0:T(8,128)(2,1)S(1)} %collective-permute-done.5), channel_id=1, source_target_pairs={{0,2},{2,4},{4,6},{6,8},{8,10},{10,12},{12,14},{14,16},{16,18},{18... | collective-permute-start | bytes 491912 | tf_op jit(solution)/shard_map/ppermute | solution.py:14
  70.6 9.9 %collective-permute-start.14 = (bf16[32,2562]{1,0:T(8,128)(2,1)S(1)}, bf16[32,2562]{1,0:T(8,128)(2,1)S(1)}, u32[]{:S(2)}, u32[]{:S(2)}) collective-permute-start(bf16[32,2562]{1,0:T(8,128)(2,1)S(1)} %collective-permute-done.13), channel_id=1, source_target_pairs={{0,30},{2,0},{4,2},{6,4},{8,6},{10,8},{12,10},{14,12},{16,14},{18,... | collective-permute-start | bytes 491912 | tf_op jit(solution)/shard_map/ppermute | solution.py:14
  78.6 9.1 %collective-permute-start.7 = (bf16[32,2562]{1,0:T(8,128)(2,1)S(1)}, bf16[32,2562]{1,0:T(8,128)(2,1)S(1)}, u32[]{:S(2)}, u32[]{:S(2)}) collective-permute-start(bf16[32,2562]{1,0:T(8,128)(2,1)S(1)} %collective-permute-done.6), channel_id=1, source_target_pairs={{0,2},{2,4},{4,6},{6,8},{8,10},{10,12},{12,14},{14,16},{16,18},{18... | collective-permute-start | bytes 491912 | tf_op jit(solution)/shard_map/ppermute | solution.py:14
  80.5 15.7 %collective-permute-start.15 = (bf16[32,2562]{1,0:T(8,128)(2,1)S(1)}, bf16[32,2562]{1,0:T(8,128)(2,1)S(1)}, u32[]{:S(2)}, u32[]{:S(2)}) collective-permute-start(bf16[32,2562]{1,0:T(8,128)(2,1)S(1)} %collective-permute-done.14), channel_id=1, source_target_pairs={{0,30},{2,0},{4,2},{6,4},{8,6},{10,8},{12,10},{14,12},{16,14},{18,... | collective-permute-start | bytes 491912 | tf_op jit(solution)/shard_map/ppermute | solution.py:14
  87.7 8.5 %collective-permute-start.8 = (bf16[32,2562]{1,0:T(8,128)(2,1)S(1)}, bf16[32,2562]{1,0:T(8,128)(2,1)S(1)}, u32[]{:S(2)}, u32[]{:S(2)}) collective-permute-start(bf16[32,2562]{1,0:T(8,128)(2,1)S(1)} %collective-permute-done.7), channel_id=1, source_target_pairs={{0,2},{2,4},{4,6},{6,8},{8,10},{10,12},{12,14},{14,16},{16,18},{18... | collective-permute-start | bytes 491912 | tf_op jit(solution)/shard_map/ppermute | solution.py:14
  105.0 30.0 %copy-start = (s32[16]{0:T(128)S(1)}, s32[16]{0:T(128)}, u32[]{:S(2)}) copy-start(s32[16]{0:T(128)} %param.9) | copy-start | bytes 196
Sparse Core Ops, SparseCore 0:
  10.0 80.5 all-gather.1
